TPU v7x, 128 devices: a whole 4x4x4 slice. The times are simulated.
128 devices in a mesh: ctx: 8 (over y, core), req: 16 (over x, z).
Axes of the slice: x: 4, y: 4, z: 4, core: 2. Of those that a mesh axis runs over, the one named last changes fastest.
Arguments:
- queries: bfloat16 [16, 512, 1024], P('req', 'ctx'), may hold values from -6 to 6
- keys: bfloat16 [16, 512, 1024], P('req', 'ctx'), may hold values from -6 to 6
- values: bfloat16 [16, 512, 2048], P('req', 'ctx'), may hold values from -6 to 6
- gate_input: bfloat16 [16, 512, 2048], P('req', 'ctx'), may hold values from -6 to 6
- beta: float32 [16, 16, 512], P('req', None, 'ctx'), may hold values from 0.05 to 1
- log_decay: float32 [16, 16, 512], P('req', None, 'ctx'), may hold values from -1 to 0
- norm_gain: float32 [128], replicated, may hold values from 0.1 to 1.9
- w_out: bfloat16 [2048, 2048], replicated, may hold values from -0.125 to 0.125
- hidden: bfloat16 [16, 512, 2048], P('req', 'ctx'), may hold values from -6 to 6
- post_gain: float32 [2048], replicated, may hold values from 0.1 to 1.9
- routes: int32 [16, 512, 10], P('req', 'ctx'), may hold values from 0 to 255, all different within a row; in each aligned block of 64 rows (0 to 63, 64 to 127, ..., all dimensions but the last counted through in order) at most 3 rows name the same one
- route_scores: float32 [16, 512, 10], P('req', 'ctx'), may hold values from 0.1 to 1
- expert_gate_up: bfloat16 [256, 2048, 1024], P(('ctx', 'req')), may hold values from -0.125 to 0.125
- expert_down: bfloat16 [256, 512, 2048], P(('ctx', 'req')), may hold values from -0.25 to 0.25
- accepted: int32 [16], P('req'), may hold values from 1 to 512
Outputs:
- layer_out: bfloat16 [16, 512, 2048], P('req', 'ctx')
- final_state: float32 [16, 16, 128, 128], P('req', 'ctx')
Inputs may be any that keep to these rules, and one draw needn't show every extreme that they name: A position's routes name different experts. Among the 64 positions of one device, no expert is named by more than 3 routes, a bound that some block reaches.
All inputs are finite; a program needn't handle non-finite values.
Results may differ from a plain program's by a relative error of at most 0.008.
Values may be sent and summed in bfloat16 or wider, within the bound.
No kernel may reach another device: no remote copies, remote signals or barrier semaphores. Data moves between devices by JAX's collectives and lax.ppermute only.
A program may use at most 128 MiB of HBM per device.

v0:
```python
import jax
import jax.numpy as jnp
from jax import lax
from jax.sharding import PartitionSpec as P

D = 2048
HK = 8
HV = 16
DK = 128
DV = 128
FFE = 512
TOPK = 10
EXP_DEV = 2


def unit_rows(x):
    x = x.astype(jnp.float32)
    return x * lax.rsqrt(jnp.sum(x * x, axis=-1, keepdims=True) + 1e-06)


def unit_lower_inverse(lower):
    highest = lax.Precision.HIGHEST
    n = lower.shape[-1]
    rows = jnp.arange(n)[:, None]
    cols = jnp.arange(n)[None, :]
    inv = None
    b = 1
    while b < n:
        sel = (rows // (2 * b) == cols // (2 * b)) & ((rows // b) % 2 == 1) & ((cols // b) % 2 == 0)
        c = jnp.where(sel, lower, 0.0)
        if inv is None:
            inv = lax.optimization_barrier(jnp.eye(n, dtype=lower.dtype) - c)
        else:
            mc = jnp.einsum("...ij,...jk->...ik", inv, c, precision=highest)
            inv = inv - jnp.einsum("...ij,...jk->...ik", mc, inv, precision=highest)
        b *= 2
    return inv


def run_experts(arrived, expert_gate_up, expert_down):
    provider_rows, count, part, width = arrived.shape
    rows = arrived.transpose(1, 0, 2, 3).reshape(count, provider_rows * part, width)
    both = jnp.einsum("erd,edf->erf", rows, expert_gate_up, preferred_element_type=jnp.float32)
    inner = (jax.nn.silu(both[..., :FFE]) * both[..., FFE:]).astype(jnp.bfloat16)
    result = jnp.einsum(
        "erf,efd->erd", inner, expert_down, preferred_element_type=jnp.float32
    ).astype(jnp.bfloat16)
    return result.reshape(count, provider_rows, part, width).transpose(1, 0, 2, 3)


def shards(
    queries,
    keys,
    values,
    gate_input,
    beta,
    log_decay,
    norm_gain,
    w_out,
    hidden,
    post_gain,
    routes,
    route_scores,
    expert_gate_up,
    expert_down,
    accepted,
):
    highest = lax.Precision.HIGHEST
    seq = queries.shape[1]
    n_ctx = lax.axis_size("ctx")
    n_req = lax.axis_size("req")
    n_dev = n_ctx * n_req
    experts = EXP_DEV * n_dev
    cap = max(2, 3 * seq * TOPK // (2 * experts))
    kh_dev = HK // n_ctx
    hv_dev = HV // n_ctx
    qw = kh_dev * DK
    vw = hv_dev * DV

    rates_decay = (
        jnp.stack([beta[0], log_decay[0]]).reshape(2, n_ctx, hv_dev, seq).transpose(1, 0, 2, 3)
    )
    hi = lax.reduce_precision(rates_decay, exponent_bits=8, mantissa_bits=7)
    rest = rates_decay - hi
    mid = lax.reduce_precision(rest, exponent_bits=8, mantissa_bits=7)
    lo = lax.reduce_precision(rest - mid, exponent_bits=8, mantissa_bits=7)
    parts = jnp.stack([hi, mid, lo], axis=1).astype(jnp.bfloat16).reshape(n_ctx, 1, -1)
    width = 2 * qw + 2 * vw
    packed = jnp.concatenate(
        [
            jnp.concatenate(
                [
                    queries[0].reshape(seq, n_ctx, qw),
                    keys[0].reshape(seq, n_ctx, qw),
                    values[0].reshape(seq, n_ctx, vw),
                    gate_input[0].reshape(seq, n_ctx, vw),
                ],
                axis=2,
            ).transpose(1, 0, 2),
            jnp.pad(parts, ((0, 0), (0, 0), (0, width - parts.shape[-1]))),
        ],
        axis=1,
    )
    got = lax.all_to_all(packed, "ctx", 0, 0, tiled=True)
    arrived = got[:, :seq]
    rd = (
        got[:, seq, : parts.shape[-1]]
        .astype(jnp.float32)
        .reshape(n_ctx, 3, 2, hv_dev, seq)
    )
    rd = (rd[:, 0] + rd[:, 1]) + rd[:, 2]
    rates = rd[:, 0].transpose(1, 0, 2)
    gamma = jnp.cumsum(rd[:, 1].transpose(1, 0, 2), axis=-1)
    qc = unit_rows(arrived[..., :qw]) * DK ** (-0.5)
    kc = unit_rows(arrived[..., qw : 2 * qw])
    vc = (
        arrived[..., 2 * qw : 2 * qw + vw]
        .astype(jnp.float32)
        .reshape(n_ctx, seq, hv_dev, DV)
        .transpose(2, 0, 1, 3)
    )
    gc = arrived[..., 2 * qw + vw :].reshape(n_ctx, seq, hv_dev, DV)

    ordinals = jnp.arange(seq)
    before = ordinals[:, None] > ordinals[None, :]
    upto = ordinals[:, None] >= ordinals[None, :]
    spans = gamma[..., :, None] - gamma[..., None, :]
    pair_decay = jnp.exp(jnp.where(upto, spans, 0.0))
    key_key = jnp.einsum("ntd,nsd->nts", kc, kc, precision=highest)
    lower = jnp.where(before, pair_decay * key_key[None] * rates[..., None, :], 0.0)
    inverse = unit_lower_inverse(lower)
    growth = jnp.exp(gamma)
    right = jnp.concatenate(
        [vc, growth[..., None] * jnp.broadcast_to(kc[None], vc.shape)], axis=-1
    )
    solved = jnp.einsum("hnts,hnsf->hntf", inverse, right, precision=highest)
    solved_values = solved[..., :DV]
    solved_keys = solved[..., DV:]
    tail = rates * jnp.exp(gamma[..., -1:] - gamma)
    weighted = (kc[None] * tail[..., None]).reshape(hv_dev * n_ctx, seq, DK)
    carried = jnp.einsum(
        "btd,btf->bdf", weighted, solved.reshape(hv_dev * n_ctx, seq, DV + DK), precision=highest
    ).reshape(hv_dev, n_ctx, DK, DV + DK)
    identity = jnp.eye(DK, dtype=jnp.float32)
    transfer = growth[..., -1, None, None] * identity - carried[..., DV:]
    offset = carried[..., :DV]
    state = jnp.zeros((hv_dev, DK, DV), jnp.float32)
    states = [state]
    for n in range(n_ctx - 1):
        state = offset[:, n] + jnp.einsum(
            "hde,hef->hdf", transfer[:, n], state, precision=highest
        )
        states.append(state)
    states = jnp.stack(states, axis=1)
    pseudo = solved_values - jnp.einsum("hntd,hnde->hnte", solved_keys, states, precision=highest)
    query_key = jnp.einsum("ntd,nsd->nts", qc, kc, precision=highest)
    mixing = jnp.where(upto, pair_decay * query_key[None] * rates[..., None, :], 0.0)
    core = growth[..., None] * jnp.einsum("ntd,hnde->hnte", qc, states, precision=highest)
    core = core + jnp.einsum("hnts,hnse->hnte", mixing, pseudo, precision=highest)

    last = accepted[0] - 1
    chunk = last // seq
    local = last % seq
    gamma_chunk = lax.dynamic_index_in_dim(gamma, chunk, axis=1, keepdims=False)
    rates_chunk = lax.dynamic_index_in_dim(rates, chunk, axis=1, keepdims=False)
    pseudo_chunk = lax.dynamic_index_in_dim(pseudo, chunk, axis=1, keepdims=False)
    state_chunk = lax.dynamic_index_in_dim(states, chunk, axis=1, keepdims=False)
    keys_chunk = lax.dynamic_index_in_dim(kc, chunk, axis=0, keepdims=False)
    gamma_at = lax.dynamic_index_in_dim(gamma_chunk, local, axis=1, keepdims=False)
    keep = jnp.where(
        ordinals[None, :] <= local,
        rates_chunk * jnp.exp(jnp.minimum(gamma_at[:, None] - gamma_chunk, 0.0)),
        0.0,
    )
    final_state = jnp.exp(gamma_at)[:, None, None] * state_chunk + jnp.einsum(
        "td,hte->hde", keys_chunk, keep[..., None] * pseudo_chunk, precision=highest
    )
    final_state = final_state[None]

    scale = lax.rsqrt(jnp.mean(core * core, axis=-1, keepdims=True) + 1e-06)
    gating = jax.nn.silu(gc.astype(jnp.float32).transpose(2, 0, 1, 3))
    normed = (core * scale * norm_gain * gating).astype(jnp.bfloat16)
    normed = normed.transpose(1, 2, 0, 3).reshape(n_ctx, seq, vw)
    back = lax.all_to_all(normed, "ctx", 0, 0, tiled=True)
    resid = hidden[0].astype(jnp.float32) + jnp.einsum(
        "jtf,jfd->td",
        back,
        w_out.reshape(n_ctx, vw, D),
        preferred_element_type=jnp.float32,
    )
    moe_in = (
        resid * lax.rsqrt(jnp.mean(resid * resid, axis=-1, keepdims=True) + 1e-06) * post_gain
    ).astype(jnp.bfloat16)

    flat_ids = routes[0].reshape(-1)
    onehot = (flat_ids[:, None] == jnp.arange(experts, dtype=jnp.int32)[None, :]).astype(jnp.int32)
    earlier = jnp.cumsum(onehot, axis=0) - onehot
    slot = jnp.sum(earlier * onehot, axis=1)
    target = (flat_ids * cap + slot).reshape(seq, TOPK)
    slots = (
        jnp.arange(experts * cap, dtype=jnp.int32)
        .reshape(n_dev, EXP_DEV, cap)
        .transpose(0, 2, 1)
    )
    hits = target[None, None, None, :, :] == slots[..., None, None]
    dispatch = jnp.sum(jnp.where(hits, 1.0, 0.0), axis=-1).astype(jnp.bfloat16)
    outgoing_rows = jnp.einsum(
        "dcet,tf->dcef", dispatch, moe_in, preferred_element_type=jnp.float32
    ).astype(jnp.bfloat16)
    arrived_rows = lax.all_to_all(
        outgoing_rows, ("ctx", "req"), split_axis=0, concat_axis=0, tiled=True
    )
    both = jnp.einsum(
        "scex,exf->escf", arrived_rows, expert_gate_up, preferred_element_type=jnp.float32
    )
    inner = (jax.nn.silu(both[..., :FFE]) * both[..., FFE:]).astype(jnp.bfloat16)
    result = jnp.einsum(
        "escf,efx->scex", inner, expert_down, preferred_element_type=jnp.float32
    ).astype(jnp.bfloat16)
    returned = lax.all_to_all(result, ("ctx", "req"), split_axis=0, concat_axis=0, tiled=True)
    scores = route_scores[0]
    mix_weights = scores / jnp.sum(scores, axis=-1, keepdims=True)
    combine = jnp.sum(jnp.where(hits, mix_weights, 0.0), axis=-1)
    combine_hi = lax.reduce_precision(combine, exponent_bits=8, mantissa_bits=7)
    combine_lo = combine - combine_hi
    halves = jnp.concatenate([combine_hi, combine_lo], axis=-1).astype(jnp.bfloat16)
    both_out = jnp.einsum(
        "dcet,dcex->tx", halves, returned, preferred_element_type=jnp.float32
    )
    moe_out = both_out[:seq] + both_out[seq:]
    layer_out = (resid + moe_out).astype(jnp.bfloat16)[None]
    return (layer_out, final_state)


def solution(mesh):
    placed = (
        P("req", "ctx", None),
        P("req", "ctx", None),
        P("req", "ctx", None),
        P("req", "ctx", None),
        P("req", None, "ctx"),
        P("req", None, "ctx"),
        P(),
        P(),
        P("req", "ctx", None),
        P(),
        P("req", "ctx", None),
        P("req", "ctx", None),
        P(("ctx", "req"), None, None),
        P(("ctx", "req"), None, None),
        P("req"),
    )
    return jax.shard_map(
        shards,
        mesh=mesh,
        in_specs=placed,
        out_specs=(P("req", "ctx", None), P("req", "ctx", None, None)),
        check_vma=False,
    )
```

profile of v0, /device:TPU:1, one launch (start us, length us, event | category | flops | bytes accessed | tf_op | source)
XLA Modules:
  0.0 182.9 jit_solution(17554006364719144452)
XLA Ops:
  0.7 0.8 pad_maximum_fusion.2
  1.6 1.0 copy.222
  2.6 1.0 copy.223
  3.9 1.0 pad_maximum_fusion
  4.9 6.0 %all-to-all-start = ((bf16[8,65,768]{2,1,0:T(8,128)(2,1)}), bf16[8,65,768]{2,1,0:T(8,128)(2,1)S(1)}, u32[]{:S(2)}, u32[]{:S(2)}) async-start(bf16[8,65,768]{2,1,0:T(8,128)(2,1)} %pad_maximum_fusion), calls=%async_computation | async-start | bytes 1769472 | tf_op jit(solution)/shard_map/all_to_all | solution.py:104
  11.1 0.1 eq.278
  11.3 0.1 eq.274
  11.5 0.2 fusion.29
  11.9 0.2 copy.191
  12.1 0.3 fusion.33
  13.1 11.0 %all-to-all-done = bf16[8,65,768]{2,1,0:T(8,128)(2,1)S(1)} async-done(((bf16[8,65,768]{2,1,0:T(8,128)(2,1)}), bf16[8,65,768]{2,1,0:T(8,128)(2,1)S(1)}, u32[]{:S(2)}, u32[]{:S(2)}) %all-to-all-start) | async-done | bytes 798752 | tf_op jit(solution)/shard_map/all_to_all | solution.py:104
  24.3 0.6 reduce_window_sum.26
  24.9 0.2 slice_reduce_fusion
  25.1 0.2 fusion.63
  25.3 0.7 fusion.138
  26.0 0.2 select_subtract_fusion
  26.2 0.8 fusion.60
  27.1 0.6 convolution_subtract_fusion.4
  27.7 0.8 fusion.58
  28.6 0.6 convolution_subtract_fusion.3
  29.2 0.8 fusion.56
  30.1 0.6 convolution_subtract_fusion.2
  30.7 0.8 fusion.54
  31.6 0.6 convolution_subtract_fusion.1
  32.2 0.8 fusion.52
  33.1 0.6 convolution_subtract_fusion
  33.9 0.1 convert_multiply_fusion.2
  34.0 0.2 broadcast_multiply_fusion
  34.2 0.9 convert_bitcast_fusion
  35.1 0.9 copy.264
  35.9 1.0 bitcast_multiply_fusion.3
  37.0 0.1 copy.204
  37.1 2.1 %fusion.24 = f32[2,8,64,256]{3,2,1,0:T(8,128)S(1)} fusion(f32[2,8,64,64]{3,2,1,0:T(8,128)S(1)} %convolution_subtract_fusion, f32[2,8,64,128]{3,2,1,0:T(8,128)S(1)} %broadcast_multiply_fusion, f32[2,8,64,128]{3,2,1,0:T(8,128)} %bitcast.315), kind=kOutput, calls=%fused_computation.37 | convolution fusion | flops 201588736 | bytes 2359296 | tf_op jit(solution)/shard_map/hnts,hnsf->hntf/dot_general | solution.py:136
  39.2 1.9 %fusion.171 = f32[16,128,256]{2,1,0:T(8,128)S(1)} fusion(f32[16,64,128]{2,1,0:T(8,128)S(1)} %copy-done, f32[16,64,256]{2,1,0:T(8,128)S(1)} %bitcast.314), kind=kOutput, calls=%fused_computation.318 | convolution fusion | flops 402653184 | bytes 3670016 | tf_op jit(solution)/shard_map/btd,btf->bdf/dot_general | solution.py:141
  41.1 0.4 copy_subtract_fusion
  41.5 0.3 bitcast_dynamic-update-slice_fusion.5
  41.8 0.3 bitcast_dynamic-update-slice_fusion.4
  42.0 0.3 bitcast_dynamic-update-slice_fusion.3
  42.3 0.3 bitcast_dynamic-update-slice_fusion.2
  42.6 0.3 bitcast_dynamic-update-slice_fusion.1
  42.9 0.3 bitcast_dynamic-update-slice_fusion
  43.1 0.3 fusion.21
  43.4 1.1 convolution_subtract_fusion.5
  44.5 0.8 fusion.68
  45.3 0.7 fusion.65
  46.0 1.0 fusion.44
  47.0 1.1 copy_bitcast_fusion
  48.1 4.3 %all-to-all-start.1 = ((bf16[8,64,256]{2,1,0:T(8,128)(2,1)}), bf16[8,64,256]{2,1,0:T(8,128)(2,1)S(1)}, u32[]{:S(2)}, u32[]{:S(2)}) async-start(bf16[8,64,256]{2,1,0:T(8,128)(2,1)} %copy_bitcast_fusion), calls=%async_computation.1 | async-start | bytes 524288 | tf_op jit(solution)/shard_map/all_to_all | solution.py:184
  52.4 0.4 fusion.17
  52.8 6.0 %all-to-all-done.1 = bf16[8,64,256]{2,1,0:T(8,128)(2,1)S(1)} async-done(((bf16[8,64,256]{2,1,0:T(8,128)(2,1)}), bf16[8,64,256]{2,1,0:T(8,128)(2,1)S(1)}, u32[]{:S(2)}, u32[]{:S(2)}) %all-to-all-start.1) | async-done | bytes 262176 | tf_op jit(solution)/shard_map/all_to_all | solution.py:184
  58.9 5.1 %multiply_reduce_fusion = (f32[64]{0:T(128)S(1)}, f32[64,2048]{1,0:T(8,128)S(1)}) fusion(bf16[8,64,256]{2,1,0:T(8,128)(2,1)S(1)} %all-to-all-done.1, bf16[8,256,2048]{2,1,0:T(8,128)(2,1)} %bitcast.305, bf16[1,64,2048]{2,1,0:T(8,128)(2,1)S(1)} %copy-done.2), kind=kOutput, calls=%fused_computation.77 | convolution fusion | flops 537395136 | bytes 9437440 | tf_op jit(solution)/shard_map/jtf,jfd->td/dot_general | solution.py:185
  64.0 1.0 convolution_convert_fusion
  65.0 3.2 %copy.194 = bf16[128,3,2,2048]{3,2,1,0:T(2,128)(2,1)S(1)} copy(bf16[128,3,2,2048]{3,0,1,2:T(8,128)(2,1)S(1)} %convolution_convert_fusion) | data formatting | bytes 6291456 | tf_op jit(solution)/shard_map/convert_element_type | solution.py:209
  68.2 50.0 %all_to_all.20 = bf16[128,3,2,2048]{3,2,1,0:T(2,128)(2,1)S(1)} all-to-all(bf16[128,3,2,2048]{3,2,1,0:T(2,128)(2,1)S(1)} %copy.194), channel_id=1, replica_groups=mesh['ctx'=8,'req'=16] {'ctx','req'}, dimensions={0} | all-to-all | bytes 6291456 | tf_op jit(solution)/shard_map/all_to_all | solution.py:210
  118.2 6.6 %fusion = f32[2,128,3,1024]{3,1,2,0:T(8,128)S(1)} fusion(bf16[2,2048,1024]{2,1,0:T(8,128)(2,1)} %param.27, bf16[128,3,2,2048]{3,2,1,0:T(2,128)(2,1)S(1)} %all_to_all.20), kind=kOutput, calls=%fused_computation | convolution fusion | flops 3221225472 | bytes 14680064 | tf_op jit(solution)/shard_map/scex,exf->escf/dot_general | solution.py:213
  124.9 1.9 %fusion.10 = bf16[128,3,2,2048]{3,0,2,1:T(8,128)(2,1)S(1)} fusion(bf16[2,512,2048]{2,1,0:T(8,128)(2,1)S(1)} %copy-done.9, f32[2,128,3,1024]{3,1,2,0:T(8,128)S(1)} %fusion), kind=kOutput, calls=%fused_computation.9 | convolution fusion | flops 1614544896 | bytes 10485760 | tf_op jit(solution)/shard_map/escf,efx->scex/dot_general | solution.py:217
  126.8 4.9 %copy.197 = bf16[128,3,2,2048]{3,2,1,0:T(2,128)(2,1)} copy(bf16[128,3,2,2048]{3,0,2,1:T(8,128)(2,1)S(1)} %fusion.10) | data formatting | bytes 6291456 | tf_op jit(solution)/shard_map/convert_element_type | solution.py:219
  131.7 5.3 %all-to-all-start.3 = ((bf16[128,3,2,2048]{3,2,1,0:T(2,128)(2,1)}), bf16[128,3,2,2048]{3,2,1,0:T(2,128)(2,1)}, u32[]{:S(2)}, u32[]{:S(2)}) async-start(bf16[128,3,2,2048]{3,2,1,0:T(2,128)(2,1)} %copy.197), calls=%async_computation.3 | async-start | bytes 6291456 | tf_op jit(solution)/shard_map/all_to_all | solution.py:220
  137.9 0.2 fusion.157
  138.1 0.5 fusion.23
  138.6 0.8 copy.200
  139.4 38.4 %all-to-all-done.3 = bf16[128,3,2,2048]{3,2,1,0:T(2,128)(2,1)} async-done(((bf16[128,3,2,2048]{3,2,1,0:T(2,128)(2,1)}), bf16[128,3,2,2048]{3,2,1,0:T(2,128)(2,1)}, u32[]{:S(2)}, u32[]{:S(2)}) %all-to-all-start.3) | async-done | bytes 3145760 | tf_op jit(solution)/shard_map/all_to_all | solution.py:220
  177.8 3.9 %fusion.13 = f32[128,2048]{1,0:T(8,128)S(1)} fusion(bf16[128,3,2,2048]{3,2,1,0:T(2,128)(2,1)} %all-to-all-done.3, bf16[128,3,2,64]{0,3,2,1:T(8,128)(2,1)S(1)} %get-tuple-element.21, bf16[128,3,2,64]{0,3,2,1:T(8,128)(2,1)S(1)} %get-tuple-element.20), kind=kOutput, calls=%fused_computation.12 | convolution fusion | flops 403046400 | bytes 4390912 | tf_op jit(solution)/shard_map/dcet,dcex->tx/dot_general | solution.py:227
  181.7 0.8 fusion.72
  (79 shorter events, 2.2 us)
Async XLA Ops:
  0.6 3.1 %copy-start.3 = (bf16[1,64,1024]{2,1,0:T(8,128)(2,1)S(1)}, bf16[1,64,1024]{2,1,0:T(8,128)(2,1)}, u32[]{:S(2)}) copy-start(bf16[1,64,1024]{2,1,0:T(8,128)(2,1)} %param.15) | copy-start | bytes 393220
  0.6 3.1 %copy-start.4 = (bf16[1,64,1024]{2,1,0:T(8,128)(2,1)S(1)}, bf16[1,64,1024]{2,1,0:T(8,128)(2,1)}, u32[]{:S(2)}) copy-start(bf16[1,64,1024]{2,1,0:T(8,128)(2,1)} %param.16) | copy-start | bytes 393220
  3.9 7.1 %copy-start.7 = (s32[1,64,10]{1,0,2:T(1,128)S(1)}, s32[1,64,10]{1,0,2:T(1,128)}, u32[]{:S(2)}) copy-start(s32[1,64,10]{1,0,2:T(1,128)} %param.25) | copy-start | bytes 7684
  4.9 19.2 %all-to-all-start = ((bf16[8,65,768]{2,1,0:T(8,128)(2,1)}), bf16[8,65,768]{2,1,0:T(8,128)(2,1)S(1)}, u32[]{:S(2)}, u32[]{:S(2)}) async-start(bf16[8,65,768]{2,1,0:T(8,128)(2,1)} %pad_maximum_fusion), calls=%async_computation | async-start | bytes 1769472 | tf_op jit(solution)/shard_map/all_to_all | solution.py:104
  11.8 1.2 copy-start.5
  37.1 2.1 %copy-start = (f32[16,64,128]{2,1,0:T(8,128)S(1)}, f32[16,64,128]{2,1,0:T(8,128)}, u32[]{:S(2)}) copy-start(f32[16,64,128]{2,1,0:T(8,128)} %bitcast_multiply_fusion.3) | copy-start | bytes 1572868
  44.5 2.5 %copy-start.1 = (f32[8,8,2,8,128]{4,3,2,1,0:T(8,128)S(1)}, f32[8,8,2,8,128]{4,3,2,1,0:T(8,128)}, u32[]{:S(2)}) copy-start(f32[8,8,2,8,128]{4,3,2,1,0:T(8,128)} %get-tuple-element.19) | copy-start | bytes 1572868
  44.5 2.5 %copy-start.8 = (f32[128]{0:T(128)S(1)}, f32[128]{0:T(128)}, u32[]{:S(2)}) copy-start(f32[128]{0:T(128)} %param.21) | copy-start | bytes 1540
  45.9 12.9 %copy-start.2 = (bf16[1,64,2048]{2,1,0:T(8,128)(2,1)S(1)}, bf16[1,64,2048]{2,1,0:T(8,128)(2,1)}, u32[]{:S(2)}) copy-start(bf16[1,64,2048]{2,1,0:T(8,128)(2,1)} %param.23) | copy-start | bytes 786436
  48.1 10.8 %all-to-all-start.1 = ((bf16[8,64,256]{2,1,0:T(8,128)(2,1)}), bf16[8,64,256]{2,1,0:T(8,128)(2,1)S(1)}, u32[]{:S(2)}, u32[]{:S(2)}) async-start(bf16[8,64,256]{2,1,0:T(8,128)(2,1)} %copy_bitcast_fusion), calls=%async_computation.1 | async-start | bytes 524288 | tf_op jit(solution)/shard_map/all_to_all | solution.py:184
  58.9 5.1 %copy-start.6 = (f32[2048]{0:T(1024)S(1)}, f32[2048]{0:T(1024)}, u32[]{:S(2)}) copy-start(f32[2048]{0:T(1024)} %param.24) | copy-start | bytes 24580
  118.2 6.7 %copy-start.9 = (bf16[2,512,2048]{2,1,0:T(8,128)(2,1)S(1)}, bf16[2,512,2048]{2,1,0:T(8,128)(2,1)}, u32[]{:S(2)}) copy-start(bf16[2,512,2048]{2,1,0:T(8,128)(2,1)} %param.28) | copy-start | bytes 12582916
  131.7 46.1 %all-to-all-start.3 = ((bf16[128,3,2,2048]{3,2,1,0:T(2,128)(2,1)}), bf16[128,3,2,2048]{3,2,1,0:T(2,128)(2,1)}, u32[]{:S(2)}, u32[]{:S(2)}) async-start(bf16[128,3,2,2048]{3,2,1,0:T(2,128)(2,1)} %copy.197), calls=%async_computation.3 | async-start | bytes 6291456 | tf_op jit(solution)/shard_map/all_to_all | solution.py:220
where the time goes:
time: 186 us; the launch traced here: 183 us
  waiting for transfers between devices  55.4 us (30%)
  blocking collectives  50 us (27%)
  matrix products  36.4 us (20%)
  starting transfers between devices  15.5 us (8%)
  local copies, waits for them, and re-layouts  13.8 us (7%)
  other arithmetic  9.23 us (5%)
  between operations  2.55 us (1%)
    all_to_all x1, blocking collectives, shards(): lax.all_to_all(outgoing_rows, ('ctx', 'req'), split_axis=0, concat_axis=0...  50 us
    all_to_all x1, waiting for transfers between devices, shards(): lax.all_to_all(result, ('ctx', 'req'), split_axis=0, concat_axis=0, tiled...  38.4 us
    all_to_all x1, waiting for transfers between devices, shards(): got = lax.all_to_all(packed, 'ctx', 0, 0, tiled=True)  11 us
    dot_general x1, matrix products, shards(): jnp.einsum('scex,exf->escf', arrived_rows, expert_gate_up, preferred_elem...  6.65 us
    all_to_all x1, waiting for transfers between devices, shards(): back = lax.all_to_all(normed, 'ctx', 0, 0, tiled=True)  6.02 us
    all_to_all x1, starting transfers between devices, shards(): got = lax.all_to_all(packed, 'ctx', 0, 0, tiled=True)  5.96 us
    all_to_all x1, starting transfers between devices, shards(): lax.all_to_all(result, ('ctx', 'req'), split_axis=0, concat_axis=0, tiled...  5.27 us
    dot_general x1, matrix products, shards(): jnp.einsum('jtf,jfd->td', back, w_out.reshape(n_ctx, vw, D), preferred_el...  5.08 us
  transfers between devices with their start and end apart: 3, of which 3 were waited for; matrix products, arithmetic and copies ran while one was open for 2% of the time, Pallas kernels for 0%

commit v1 on v0

--- a/solution.py
+++ b/solution.py
@@ -204,12 +204,12 @@
     )
     hits = target[None, None, None, :, :] == slots[..., None, None]
     dispatch = jnp.sum(jnp.where(hits, 1.0, 0.0), axis=-1).astype(jnp.bfloat16)
-    outgoing_rows = jnp.einsum(
-        "dcet,tf->dcef", dispatch, moe_in, preferred_element_type=jnp.float32
+    outgoing_rows = jnp.dot(
+        dispatch.reshape(experts * cap, seq), moe_in, preferred_element_type=jnp.float32
     ).astype(jnp.bfloat16)
     arrived_rows = lax.all_to_all(
         outgoing_rows, ("ctx", "req"), split_axis=0, concat_axis=0, tiled=True
-    )
+    ).reshape(n_dev, cap, EXP_DEV, D)
     both = jnp.einsum(
         "scex,exf->escf", arrived_rows, expert_gate_up, preferred_element_type=jnp.float32
     )
@@ -217,7 +217,9 @@
     result = jnp.einsum(
         "escf,efx->scex", inner, expert_down, preferred_element_type=jnp.float32
     ).astype(jnp.bfloat16)
-    returned = lax.all_to_all(result, ("ctx", "req"), split_axis=0, concat_axis=0, tiled=True)
+    returned = lax.all_to_all(
+        result.reshape(experts * cap, D), ("ctx", "req"), split_axis=0, concat_axis=0, tiled=True
+    ).reshape(n_dev, cap, EXP_DEV, D)
     scores = route_scores[0]
     mix_weights = scores / jnp.sum(scores, axis=-1, keepdims=True)
     combine = jnp.sum(jnp.where(hits, mix_weights, 0.0), axis=-1)

time: 186 us -> 205 us (1.10); the launches traced: 183 us -> 204 us
  blocking collectives: 50 us -> 61.4 us
  waiting for transfers between devices: 55.4 us -> 63.6 us
  local copies, waits for them, and re-layouts: 13.8 us -> 21.2 us
  matrix products: 36.4 us -> 32.2 us
    all_to_all x0 -> x4, local copies, waits for them, and re-layouts: none -> 12.2 us  [the longest x2 7.65 us: shards(): lax.all_to_all(result.reshape(experts * cap, D), ('ctx', 'req'), split_ax...]
    all_to_all x1, blocking collectives: 50 us -> 61.4 us  [shards(): lax.all_to_all(outgoing_rows, ('ctx', 'req'), split_axis=0, concat_axis=0...]
    all_to_all x1, waiting for transfers between devices: 38.4 us -> 48.1 us  [shards(): lax.all_to_all(result.reshape(experts * cap, D), ('ctx', 'req'), split_ax...]
    convert_element_type x1, local copies, waits for them, and re-layouts: 4.94 us -> 0.4 us  [shards(): result = jnp.einsum('escf,efx->scex', inner, expert_down, preferred_eleme...]
    dot_general x1, matrix products: 3.89 us -> 0.61 us  [shards(): jnp.einsum('dcet,dcex->tx', halves, returned, preferred_element_type=jnp....]
    convert_element_type x1, local copies, waits for them, and re-layouts: 3.24 us -> 0.83 us  [shards(): dispatch = jnp.sum(jnp.where(hits, 1.0, 0.0), axis=-1).astype(jnp.bfloat16)]
    unnamed x27 -> x33, local copies, waits for them, and re-layouts: 2.95 us -> 5.02 us
  transfers between devices with their start and end apart: 3 -> 3, of which waited for: 3 -> 3; matrix products, arithmetic and copies ran while one was open for 2% -> 4% of each run, Pallas kernels for 0% -> 0%
where the time goes in v1:
time: 205 us; the launch traced here: 204 us
  waiting for transfers between devices  63.6 us (31%)
  blocking collectives  61.4 us (30%)
  matrix products  32.2 us (16%)
  local copies, waits for them, and re-layouts  21.2 us (10%)
  starting transfers between devices  15.5 us (8%)
  other arithmetic  8.3 us (4%)
  between operations  2.14 us (1%)
    all_to_all x1, blocking collectives, shards(): lax.all_to_all(outgoing_rows, ('ctx', 'req'), split_axis=0, concat_axis=0...  61.4 us
    all_to_all x1, waiting for transfers between devices, shards(): lax.all_to_all(result.reshape(experts * cap, D), ('ctx', 'req'), split_ax...  48.1 us
    all_to_all x1, waiting for transfers between devices, shards(): got = lax.all_to_all(packed, 'ctx', 0, 0, tiled=True)  11 us
    all_to_all x2, local copies, waits for them, and re-layouts, shards(): lax.all_to_all(result.reshape(experts * cap, D), ('ctx', 'req'), split_ax...  7.65 us
    dot_general x1, matrix products, shards(): jnp.einsum('scex,exf->escf', arrived_rows, expert_gate_up, preferred_elem...  6 us
    all_to_all x1, starting transfers between devices, shards(): got = lax.all_to_all(packed, 'ctx', 0, 0, tiled=True)  5.96 us
    all_to_all x1, starting transfers between devices, shards(): lax.all_to_all(result.reshape(experts * cap, D), ('ctx', 'req'), split_ax...  5.22 us
    dot_general x1, matrix products, shards(): jnp.einsum('jtf,jfd->td', back, w_out.reshape(n_ctx, vw, D), preferred_el...  5.11 us
  transfers between devices with their start and end apart: 3, of which 3 were waited for; matrix products, arithmetic and copies ran while one was open for 4% of the time, Pallas kernels for 0%

profile of v1, /device:TPU:1, one launch (start us, length us, event | category | flops | bytes accessed | tf_op | source)
XLA Modules:
  0.0 204.4 jit_solution(16077242131389426599)
XLA Ops:
  0.6 0.8 pad_maximum_fusion.2
  1.6 0.9 copy.224
  2.5 0.9 copy.225
  3.5 1.0 copy.226
  4.8 1.0 pad_maximum_fusion
  5.8 6.0 %all-to-all-start = ((bf16[8,65,768]{2,1,0:T(8,128)(2,1)}), bf16[8,65,768]{2,1,0:T(8,128)(2,1)S(1)}, u32[]{:S(2)}, u32[]{:S(2)}) async-start(bf16[8,65,768]{2,1,0:T(8,128)(2,1)} %pad_maximum_fusion), calls=%async_computation | async-start | bytes 1769472 | tf_op jit(solution)/shard_map/all_to_all | solution.py:104
  12.4 0.2 fusion.24
  12.7 0.2 copy.194
  12.9 0.3 fusion.29
  14.0 11.0 %all-to-all-done = bf16[8,65,768]{2,1,0:T(8,128)(2,1)S(1)} async-done(((bf16[8,65,768]{2,1,0:T(8,128)(2,1)}), bf16[8,65,768]{2,1,0:T(8,128)(2,1)S(1)}, u32[]{:S(2)}, u32[]{:S(2)}) %all-to-all-start) | async-done | bytes 798752 | tf_op jit(solution)/shard_map/all_to_all | solution.py:104
  25.1 0.6 reduce_window_sum.26
  26.2 0.2 fusion.59
  26.4 0.7 fusion.131
  27.1 0.2 select_subtract_fusion
  27.3 0.8 fusion.56
  28.2 0.6 convolution_subtract_fusion.4
  28.8 0.8 fusion.54
  29.7 0.6 convolution_subtract_fusion.3
  30.3 0.8 fusion.52
  31.2 0.6 convolution_subtract_fusion.2
  31.8 0.8 fusion.50
  32.7 0.6 convolution_subtract_fusion.1
  33.3 0.8 fusion.48
  34.2 0.6 convolution_subtract_fusion
  35.0 0.2 broadcast_multiply_fusion
  35.2 0.2 bitcast_multiply_fusion.3
  35.5 1.0 fusion.19
  36.5 1.9 fusion.165
  38.4 0.4 copy_subtract_fusion
  38.8 0.3 bitcast_dynamic-update-slice_fusion.5
  39.1 0.3 bitcast_dynamic-update-slice_fusion.4
  39.4 0.3 bitcast_dynamic-update-slice_fusion.3
  39.6 0.3 bitcast_dynamic-update-slice_fusion.2
  39.9 0.3 bitcast_dynamic-update-slice_fusion.1
  40.2 0.3 bitcast_dynamic-update-slice_fusion
  40.5 0.3 fusion.16
  40.7 1.1 convolution_subtract_fusion.5
  41.8 0.7 fusion.61
  42.5 0.8 fusion.64
  43.3 1.0 fusion.40
  44.3 1.0 copy_bitcast_fusion
  45.4 4.3 %all-to-all-start.1 = ((bf16[8,64,256]{2,1,0:T(8,128)(2,1)}), bf16[8,64,256]{2,1,0:T(8,128)(2,1)S(1)}, u32[]{:S(2)}, u32[]{:S(2)}) async-start(bf16[8,64,256]{2,1,0:T(8,128)(2,1)} %copy_bitcast_fusion), calls=%async_computation.1 | async-start | bytes 524288 | tf_op jit(solution)/shard_map/all_to_all | solution.py:184
  49.8 1.1 fusion.12
  50.8 0.8 copy.196
  51.7 4.5 %all-to-all-done.1 = bf16[8,64,256]{2,1,0:T(8,128)(2,1)S(1)} async-done(((bf16[8,64,256]{2,1,0:T(8,128)(2,1)}), bf16[8,64,256]{2,1,0:T(8,128)(2,1)S(1)}, u32[]{:S(2)}, u32[]{:S(2)}) %all-to-all-start.1) | async-done | bytes 262176 | tf_op jit(solution)/shard_map/all_to_all | solution.py:184
  56.2 5.1 %multiply_reduce_fusion = (f32[64]{0:T(128)S(1)}, f32[64,2048]{1,0:T(8,128)S(1)}) fusion(bf16[8,64,256]{2,1,0:T(8,128)(2,1)S(1)} %all-to-all-done.1, bf16[8,256,2048]{2,1,0:T(8,128)(2,1)} %bitcast.310, bf16[1,64,2048]{2,1,0:T(8,128)(2,1)S(1)} %copy-done.6), kind=kOutput, calls=%fused_computation.75 | convolution fusion | flops 537395136 | bytes 9437440 | tf_op jit(solution)/shard_map/jtf,jfd->td/dot_general | solution.py:185
  61.3 0.8 copy-done.1
  62.1 1.0 convolution_convert_fusion
  63.1 2.8 %all_to_all.20 = bf16[128,6,2048]{2,1,0:T(8,128)(2,1)} reshape(bf16[768,2048]{1,0:T(8,128)(2,1)S(1)} %convolution_convert_fusion) | data formatting | bytes 6291456 | tf_op jit(solution)/shard_map/all_to_all | solution.py:210
  66.0 61.4 %all_to_all.28 = bf16[128,6,2048]{2,1,0:T(8,128)(2,1)S(1)} all-to-all(bf16[128,6,2048]{2,1,0:T(8,128)(2,1)} %all_to_all.20), channel_id=1, replica_groups=mesh['ctx'=8,'req'=16] {'ctx','req'}, dimensions={0} | all-to-all | bytes 6291456 | tf_op jit(solution)/shard_map/all_to_all | solution.py:210
  127.4 1.7 copy.197
  129.2 6.0 %fusion = f32[2,128,3,1024]{3,1,2,0:T(8,128)S(1)} fusion(bf16[2,2048,1024]{2,1,0:T(8,128)(2,1)} %param.27, bf16[128,3,2,2048]{3,0,2,1:T(8,128)(2,1)S(1)} %bitcast.322), kind=kOutput, calls=%fused_computation | convolution fusion | flops 3221225472 | bytes 14680064 | tf_op jit(solution)/shard_map/scex,exf->escf/dot_general | solution.py:213
  135.2 1.9 fusion.8
  137.0 0.4 copy.199
  137.5 3.7 %copy.200 = bf16[128,6,2048]{2,1,0:T(8,128)(2,1)} copy(bf16[128,6,2048]{2,0,1:T(8,128)(2,1)S(1)} %bitcast.311) | data formatting | bytes 6291456 | tf_op jit(solution)/shard_map/all_to_all | solution.py:220
  141.2 5.2 %all-to-all-start.3 = ((bf16[128,6,2048]{2,1,0:T(8,128)(2,1)}), bf16[128,6,2048]{2,1,0:T(8,128)(2,1)}, u32[]{:S(2)}, u32[]{:S(2)}) async-start(bf16[128,6,2048]{2,1,0:T(8,128)(2,1)} %copy.200), calls=%async_computation.3 | async-start | bytes 8388608 | tf_op jit(solution)/shard_map/all_to_all | solution.py:220
  147.2 0.9 dynamic-slice_bitcast_fusion
  148.5 1.3 fusion.18
  149.8 0.8 copy.203
  150.6 48.1 %all-to-all-done.3 = bf16[128,6,2048]{2,1,0:T(8,128)(2,1)} async-done(((bf16[128,6,2048]{2,1,0:T(8,128)(2,1)}), bf16[128,6,2048]{2,1,0:T(8,128)(2,1)}, u32[]{:S(2)}, u32[]{:S(2)}) %all-to-all-start.3) | async-done | bytes 3145760 | tf_op jit(solution)/shard_map/all_to_all | solution.py:220
  198.6 3.9 %copy.201 = bf16[128,6,2048]{2,0,1:T(8,128)(2,1)S(1)} copy(bf16[128,6,2048]{2,1,0:T(8,128)(2,1)} %all-to-all-done.3) | data formatting | bytes 6291456 | tf_op jit(solution)/shard_map/all_to_all | solution.py:220
  202.6 0.6 convolution_bitcast_fusion
  203.2 0.4 copy-done.2
  203.6 0.8 fusion.66
  (89 shorter events, 3.2 us)
Async XLA Ops:
  0.6 3.9 %copy-start.7 = (bf16[1,64,2048]{2,1,0:T(8,128)(2,1)S(1)}, bf16[1,64,2048]{2,1,0:T(8,128)(2,1)}, u32[]{:S(2)}) copy-start(bf16[1,64,2048]{2,1,0:T(8,128)(2,1)} %param.18) | copy-start | bytes 786436
  4.8 7.1 %copy-start.10 = (s32[1,64,10]{1,0,2:T(1,128)S(1)}, s32[1,64,10]{1,0,2:T(1,128)}, u32[]{:S(2)}) copy-start(s32[1,64,10]{1,0,2:T(1,128)} %param.25) | copy-start | bytes 7684
  5.8 19.2 %all-to-all-start = ((bf16[8,65,768]{2,1,0:T(8,128)(2,1)}), bf16[8,65,768]{2,1,0:T(8,128)(2,1)S(1)}, u32[]{:S(2)}, u32[]{:S(2)}) async-start(bf16[8,65,768]{2,1,0:T(8,128)(2,1)} %pad_maximum_fusion), calls=%async_computation | async-start | bytes 1769472 | tf_op jit(solution)/shard_map/all_to_all | solution.py:104
  12.6 1.2 copy-start.8
  40.7 2.5 %copy-start = (f32[2,8,128,128]{3,2,0,1:T(8,128)}, f32[2,8,128,128]{3,2,0,1:T(8,128)S(1)}, u32[]{:S(2)}) copy-start(f32[2,8,128,128]{3,2,0,1:T(8,128)S(1)} %fusion.16) | copy-start | bytes 3145732
  41.8 3.6 %copy-start.3 = (f32[2,8,64,128]{3,2,1,0:T(8,128)}, f32[2,8,64,128]{3,2,1,0:T(8,128)S(1)}, u32[]{:S(2)}) copy-start(f32[2,8,64,128]{3,2,1,0:T(8,128)S(1)} %convolution_subtract_fusion.5) | copy-start | bytes 1572868
  41.8 2.5 %copy-start.11 = (f32[128]{0:T(128)S(1)}, f32[128]{0:T(128)}, u32[]{:S(2)}) copy-start(f32[128]{0:T(128)} %param.21) | copy-start | bytes 1540
  43.3 12.9 %copy-start.6 = (bf16[1,64,2048]{2,1,0:T(8,128)(2,1)S(1)}, bf16[1,64,2048]{2,1,0:T(8,128)(2,1)}, u32[]{:S(2)}) copy-start(bf16[1,64,2048]{2,1,0:T(8,128)(2,1)} %param.23) | copy-start | bytes 786436
  45.4 10.8 %all-to-all-start.1 = ((bf16[8,64,256]{2,1,0:T(8,128)(2,1)}), bf16[8,64,256]{2,1,0:T(8,128)(2,1)S(1)}, u32[]{:S(2)}, u32[]{:S(2)}) async-start(bf16[8,64,256]{2,1,0:T(8,128)(2,1)} %copy_bitcast_fusion), calls=%async_computation.1 | async-start | bytes 524288 | tf_op jit(solution)/shard_map/all_to_all | solution.py:184
  56.2 5.9 %copy-start.4 = (bf16[128,3,2,64]{3,2,1,0:T(2,128)(2,1)S(1)}, bf16[128,3,2,64]{3,2,1,0:T(2,128)(2,1)}, u32[]{:S(2)}) copy-start(bf16[128,3,2,64]{3,2,1,0:T(2,128)(2,1)} %copy.196) | copy-start | bytes 294916
  56.2 5.9 %copy-start.9 = (f32[2048]{0:T(1024)S(1)}, f32[2048]{0:T(1024)}, u32[]{:S(2)}) copy-start(f32[2048]{0:T(1024)} %param.24) | copy-start | bytes 24580
  61.3 0.8 copy-start.1
  129.1 6.0 %copy-start.12 = (bf16[2,512,2048]{2,1,0:T(8,128)(2,1)S(1)}, bf16[2,512,2048]{2,1,0:T(8,128)(2,1)}, u32[]{:S(2)}) copy-start(bf16[2,512,2048]{2,1,0:T(8,128)(2,1)} %param.28) | copy-start | bytes 12582916
  141.2 5.9 %copy-start.5 = (f32[128,3,2,64]{0,3,2,1:T(8,128)S(1)}, f32[128,3,2,64]{0,3,2,1:T(8,128)}, u32[]{:S(2)}) copy-start(f32[128,3,2,64]{0,3,2,1:T(8,128)} %get-tuple-element.14) | copy-start | bytes 589828
  141.2 57.4 %all-to-all-start.3 = ((bf16[128,6,2048]{2,1,0:T(8,128)(2,1)}), bf16[128,6,2048]{2,1,0:T(8,128)(2,1)}, u32[]{:S(2)}, u32[]{:S(2)}) async-start(bf16[128,6,2048]{2,1,0:T(8,128)(2,1)} %copy.200), calls=%async_computation.3 | async-start | bytes 8388608 | tf_op jit(solution)/shard_map/all_to_all | solution.py:220
  202.6 1.0 copy-start.2
